TPU v7x, 256 devices: a whole 4x4x8 slice. The times are simulated.
256 devices in a mesh: sec: 16 (over x, y), vel: 16 (over z, core).
Axes of the slice: x: 4, y: 4, z: 8, core: 2. Of those that a mesh axis runs over, the one named last changes fastest.
Arguments:
- distribution: float32 [13824, 4096], P('vel', 'sec'), may hold values from -6 to 6
- collision: float32 [4096], P('sec'), may hold values from 0.05 to 2
- lower_blocks: float32 [25, 4096], P(None, 'sec'), may hold values from -0.6 to 0.6
- upper_blocks: float32 [25, 4096], P(None, 'sec'), may hold values from -0.6 to 0.6
- diag_inverse: float32 [25, 4096], P(None, 'sec'), may hold values from -0.2 to 1.4
Outputs:
- new_distribution: float32 [13824, 4096], P('vel', 'sec')
- macro: float32 [5, 4096], P(None, 'sec')
All inputs are finite; a program needn't handle non-finite values.
Results may differ from a plain program's by a relative error of at most 0.0003.
Values sent between devices are 32-bit elements; how exact they have to be, the bound alone decides.
No kernel may reach another device: no remote copies, remote signals or barrier semaphores. Data moves between devices by JAX's collectives and lax.ppermute only.
A program may use at most 64 MiB of HBM per device.

v0:
```python
import math
import jax
import jax.numpy as jnp
import numpy as np
from jax import lax
from jax.sharding import PartitionSpec as P

NXI = 24
TUBES = 128
JACOBI = 4
NEWTON = 2
HIGH = lax.Precision.HIGHEST
pseudo_rate = 1.0


def passed_along(block, axis, distance):
    devices = range(lax.axis_size(axis))
    route = [(i - distance, i) for i in devices if i - distance in devices]
    return lax.ppermute(block, axis, route)


def extended(array, sides, width):
    for axis, dim in sides:
        count, length = (lax.axis_size(axis), array.shape[dim])
        up = [(i, (i + 1) % count) for i in range(count - 1)]
        down = [(j, i) for i, j in up]
        last = lax.slice_in_dim(array, length - width, length, axis=dim)
        first = lax.slice_in_dim(array, 0, width, axis=dim)
        before = lax.ppermute(last, axis, up)
        after = lax.ppermute(first, axis, down)
        array = jnp.concatenate([before, array, after], axis=dim)
    return array


def hermite_rule(count):
    quarter = math.pi ** (-0.25)
    found = []
    last_slope = 1.0
    for index in range(count // 2):
        if index == 0:
            guess = math.sqrt(2.0 * count + 1.0) - 1.85575 * (2.0 * count + 1.0) ** (-0.16667)
        elif index == 1:
            guess = guess - 1.14 * count**0.426 / guess
        elif index == 2:
            guess = 1.86 * guess - 0.86 * found[0][0]
        elif index == 3:
            guess = 1.91 * guess - 0.91 * found[1][0]
        else:
            guess = 2.0 * guess - found[index - 2][0]
        for repeat in range(60):
            current = quarter
            previous = 0.0
            for order in range(count):
                older = previous
                previous = current
                current = (
                    guess * math.sqrt(2.0 / (order + 1)) * previous
                    - math.sqrt(order / (order + 1.0)) * older
                )
            last_slope = math.sqrt(2.0 * count) * previous
            guess = guess - current / last_slope
        found.append((guess, 2.0 / (last_slope * last_slope)))
    positive = found[::-1]
    points = [-pair[0] for pair in found] + [pair[0] for pair in positive]
    weights = [pair[1] for pair in found] + [pair[1] for pair in positive]
    return (np.array(points), np.array(weights))


def node_tables(axis_points):
    points, weights = hermite_rule(axis_points)
    node_index = np.arange(axis_points**3)
    idx_x = node_index % axis_points
    idx_z = node_index // axis_points % axis_points
    idx_y = node_index // (axis_points * axis_points)
    along_x = points[idx_x]
    along_y = points[idx_y]
    along_z = points[idx_z]
    node_weight = weights[idx_x] * weights[idx_y] * weights[idx_z] / math.pi**1.5
    energy = along_x**2 + along_y**2 + along_z**2 - 1.5
    moment_basis = np.stack([along_x * 0.0 + 1.0, along_x, along_y, along_z, energy])
    norm_scale = np.array([1.0, 0.5, 0.5, 0.5, 1.5])
    return (
        along_x,
        node_weight,
        moment_basis * node_weight[None, :],
        moment_basis / norm_scale[:, None],
    )


def apply_block(matrices, vector):
    shaped = matrices.reshape((5, 5) + vector.shape[1:])
    return jnp.sum(shaped * vector[None], axis=1)


def affine_combine(earlier_map, later_map):
    return (later_map[0] * earlier_map[0], later_map[0] * earlier_map[1] + later_map[1])


def newton_sums(loaded, signed, shift_mass, shift_flow):
    growth = jnp.exp(shift_mass + shift_flow * signed)
    scaled = loaded * growth
    excess = loaded * (growth - 1.0)
    return jnp.stack(
        [
            jnp.sum(scaled),
            jnp.sum(scaled * signed),
            jnp.sum(scaled * signed * signed),
            jnp.sum(excess),
            jnp.sum(excess * signed),
        ]
    )


def newton_update(shift_mass, shift_flow, sums, goal_mass, goal_flow):
    resid_mass = sums[3] - goal_mass
    resid_flow = sums[4] - goal_flow
    determinant = sums[0] * sums[2] - sums[1] * sums[1]
    new_mass = shift_mass - (sums[2] * resid_mass - sums[1] * resid_flow) / determinant
    new_flow = shift_flow - (sums[0] * resid_flow - sums[1] * resid_mass) / determinant
    return (new_mass, new_flow)


def body(distribution, collision, lower_blocks, upper_blocks, diag_inverse):
    node_count = distribution.shape[0]
    cell_count = distribution.shape[1]
    length = cell_count // TUBES
    node_rows = node_count // NXI
    half_nodes = NXI // 2
    along_x, node_weight, weighted_np, rebuild_np = node_tables(NXI)
    all_signed = jnp.asarray(along_x, jnp.float32)
    all_mass = jnp.asarray(node_weight, jnp.float32)
    offset = lax.axis_index("vel") * node_count
    weighted = lax.dynamic_slice_in_dim(
        jnp.asarray(weighted_np, jnp.float32), offset, node_count, 1
    )
    rebuild = lax.dynamic_slice_in_dim(jnp.asarray(rebuild_np, jnp.float32), offset, node_count, 1)
    signed = lax.dynamic_slice_in_dim(all_signed, offset, node_count, 0)
    node_mass = lax.dynamic_slice_in_dim(all_mass, offset, node_count, 0)
    old_moments = lax.psum(jnp.dot(weighted, distribution, precision=HIGH), "vel")
    target = jnp.dot(rebuild.T, old_moments, precision=HIGH)
    total_length = length * lax.axis_size("sec")
    thickness = collision.reshape(1, 1, length, TUBES)
    node_speed = jnp.abs(signed).reshape(node_rows, NXI, 1, 1)
    denominator = node_speed * total_length + thickness + pseudo_rate
    carry_rate = node_speed * total_length / denominator
    drive_term = (
        thickness * target.reshape(node_rows, NXI, length, TUBES)
        + pseudo_rate * distribution.reshape(node_rows, NXI, length, TUBES)
    ) / denominator
    prod_neg, local_neg = lax.associative_scan(
        affine_combine,
        (carry_rate[:, :half_nodes], drive_term[:, :half_nodes]),
        reverse=True,
        axis=2,
    )
    prod_pos, local_pos = lax.associative_scan(
        affine_combine, (carry_rate[:, half_nodes:], drive_term[:, half_nodes:]), axis=2
    )
    summary_pos = (prod_pos[:, :, -1], local_pos[:, :, -1])
    summary_neg = (prod_neg[:, :, 0], local_neg[:, :, 0])

    def relay(turn_index, inflows):
        out_pos = summary_pos[0] * inflows[0] + summary_pos[1]
        out_neg = summary_neg[0] * inflows[1] + summary_neg[1]
        return (passed_along(out_pos, "sec", 1), passed_along(out_neg, "sec", -1))

    start_flows = (jnp.zeros_like(summary_pos[1]), jnp.zeros_like(summary_neg[1]))
    inflow_pos, inflow_neg = lax.fori_loop(0, lax.axis_size("sec") - 1, relay, start_flows)
    field_neg = local_neg + prod_neg * inflow_neg[:, :, None, :]
    field_pos = local_pos + prod_pos * inflow_pos[:, :, None, :]
    half_field = jnp.concatenate([field_neg, field_pos], axis=1).reshape(node_count, cell_count)
    half_moments = lax.psum(jnp.dot(weighted, half_field, precision=HIGH), "vel")
    residual = (half_moments - old_moments).reshape(5, length, TUBES)
    lower_r = lower_blocks.reshape(25, length, TUBES)
    upper_r = upper_blocks.reshape(25, length, TUBES)
    inverse_r = diag_inverse.reshape(25, length, TUBES)
    correction = apply_block(inverse_r, residual)
    for sweep_index in range(JACOBI):
        padded = extended(correction, (("sec", 1),), 1)
        correction = apply_block(
            inverse_r,
            residual - apply_block(lower_r, padded[:, :-2]) - apply_block(upper_r, padded[:, 2:]),
        )
    correction = correction.reshape(5, cell_count)
    macro = half_moments + correction
    synthetic = half_field + jnp.dot(rebuild.T, correction, precision=HIGH)
    local_totals = jnp.sum(old_moments - macro, axis=1)[0:2]
    magnitude = jnp.sum(jnp.abs(synthetic), axis=1)
    shift_mass = jnp.zeros((), jnp.float32)
    shift_flow = jnp.zeros((), jnp.float32)
    goals = lax.psum(local_totals, "sec")
    loaded = node_mass * magnitude
    for newton_turn in range(NEWTON):
        sums = lax.psum(newton_sums(loaded, signed, shift_mass, shift_flow), ("sec", "vel"))
        shift_mass, shift_flow = newton_update(shift_mass, shift_flow, sums, goals[0], goals[1])
    growth = jnp.exp(shift_mass + shift_flow * signed)
    new_distribution = synthetic + jnp.abs(synthetic) * (growth[:, None] - 1.0)
    return (new_distribution, macro)


def solution(mesh):
    in_specs = (P("vel", "sec"), P("sec"), P(None, "sec"), P(None, "sec"), P(None, "sec"))
    out_specs = (P("vel", "sec"), P(None, "sec"))
    return jax.shard_map(body, mesh=mesh, in_specs=in_specs, out_specs=out_specs, check_vma=False)
```

profile of v0, /device:TPU:1, one launch (start us, length us, event | category | flops | bytes accessed | tf_op | source)
XLA Modules:
  0.0 529.8 jit_solution(13319355678150819827)
XLA Ops:
  3.6 27.9 %psum.35 = f32[5,256]{1,0:T(8,128)S(1)} all-reduce(f32[5,256]{1,0:T(8,128)S(1)} %fusion.12), channel_id=1, replica_groups=mesh['sec'=16,'vel'=16] {'vel'}, use_global_device_ids=true, to_apply=%region_0.0 | all-reduce | flops 1280 | bytes 10240 | tf_op jit(solution)/shard_map/psum | solution.py:139
  44.4 185.1 %while.12 = (s32[]{:T(128)}, f32[36,12,128]{2,1,0:T(8,128)S(1)}, f32[36,12,128]{2,1,0:T(8,128)S(1)}, f32[36,12,128]{2,1,0:T(8,128)S(1)}, f32[36,12,128]{2,1,0:T(...) while((s32[]{:T(128)}, f32[36,12,128]{2,1,0:T(8,128)S(1)}, ...), condition=%wide.region_2.0_spmd, body=%wide.region_1.0_spmd.sunk | while | flops 221186 | bytes 3539109 | solution.py:168
  66.4 4.4 collective-permute-start
  78.4 4.0 collective-permute-start
  90.1 4.0 collective-permute-start
  109.1 4.0 collective-permute-done.1
  113.1 3.9 collective-permute-start
  121.7 4.2 collective-permute-done.1
  131.0 4.3 collective-permute-done
  135.3 4.4 collective-permute-done.1
  144.9 5.2 collective-permute-done
  150.1 4.2 collective-permute-done.1
  159.6 4.3 collective-permute-done
  167.8 4.8 collective-permute-start
  181.7 4.3 collective-permute-start
  194.1 4.3 collective-permute-start
  206.0 4.0 collective-permute-start
  217.6 4.3 collective-permute-start
  232.6 44.9 %psum.36 = f32[5,256]{1,0:T(8,128)S(1)} all-reduce(f32[5,256]{1,0:T(8,128)S(1)} %fusion), channel_id=1, replica_groups=mesh['sec'=16,'vel'=16] {'vel'}, use_global_device_ids=true, to_apply=%region_3.0 | all-reduce | flops 1280 | bytes 10240 | tf_op jit(solution)/shard_map/psum | solution.py:172
  294.3 4.0 collective-permute-start.6
  302.8 4.0 collective-permute-start.8
  314.0 30.6 %psum.38 = f32[2]{0:T(128)S(1)} all-reduce(f32[2]{0:T(128)S(1)} %bitcast.57), channel_id=1, replica_groups=mesh['sec'=16,'vel'=16] {'sec'}, use_global_device_ids=true, to_apply=%region_25.0 | all-reduce | flops 2 | bytes 16 | tf_op jit(solution)/shard_map/psum | solution.py:191
  349.9 82.5 %psum.37 = f32[5]{0:T(128)S(1)} all-reduce(f32[5]{0:T(128)S(1)} %stack.41), channel_id=1, replica_groups=mesh['sec'=16,'vel'=16] {'sec','vel'}, use_global_device_ids=true, to_apply=%region_23.0 | all-reduce | flops 5 | bytes 40 | tf_op jit(solution)/shard_map/psum | solution.py:194
  445.4 74.4 %psum.39 = f32[5]{0:T(128)S(1)} all-reduce(f32[5]{0:T(128)S(1)} %stack.47), channel_id=1, replica_groups=mesh['sec'=16,'vel'=16] {'sec','vel'}, use_global_device_ids=true, to_apply=%region_31.0 | all-reduce | flops 5 | bytes 40 | tf_op jit(solution)/shard_map/psum | solution.py:194
  (166 shorter events, 175.8 us)
Async XLA Ops:
  47.8 7.5 %collective-permute-start.1 = (f32[36,12,128]{2,1,0:T(8,128)S(1)}, f32[36,12,128]{2,1,0:T(8,128)S(1)}, u32[]{:S(2)}, u32[]{:S(2)}) collective-permute-start(f32[36,12,128]{2,1,0:T(8,128)S(1)} %multiply_add_fusion.7), channel_id=1, source_target_pairs={{16,0},{32,16},{48,32},{64,48},{80,64},{96,80},{112,96},{128,112},... | collective-permute-start | bytes 663560 | tf_op jit(solution)/shard_map/while/body/eval_jaxpr/ppermute | solution.py:19
  58.9 7.5 %collective-permute-start.1 = (f32[36,12,128]{2,1,0:T(8,128)S(1)}, f32[36,12,128]{2,1,0:T(8,128)S(1)}, u32[]{:S(2)}, u32[]{:S(2)}) collective-permute-start(f32[36,12,128]{2,1,0:T(8,128)S(1)} %multiply_add_fusion.7), channel_id=1, source_target_pairs={{16,0},{32,16},{48,32},{64,48},{80,64},{96,80},{112,96},{128,112},... | collective-permute-start | bytes 663560 | tf_op jit(solution)/shard_map/while/body/eval_jaxpr/ppermute | solution.py:19
  66.4 8.1 %collective-permute-start = (f32[36,12,128]{2,1,0:T(8,128)S(1)}, f32[36,12,128]{2,1,0:T(8,128)S(1)}, u32[]{:S(2)}, u32[]{:S(2)}) collective-permute-start(f32[36,12,128]{2,1,0:T(8,128)S(1)} %multiply_add_fusion.6), channel_id=1, source_target_pairs={{0,16},{16,32},{32,48},{48,64},{64,80},{80,96},{96,112},{112,128},... | collective-permute-start | bytes 663560 | tf_op jit(solution)/shard_map/while/body/eval_jaxpr/ppermute | solution.py:19
  70.9 7.5 %collective-permute-start.1 = (f32[36,12,128]{2,1,0:T(8,128)S(1)}, f32[36,12,128]{2,1,0:T(8,128)S(1)}, u32[]{:S(2)}, u32[]{:S(2)}) collective-permute-start(f32[36,12,128]{2,1,0:T(8,128)S(1)} %multiply_add_fusion.7), channel_id=1, source_target_pairs={{16,0},{32,16},{48,32},{64,48},{80,64},{96,80},{112,96},{128,112},... | collective-permute-start | bytes 663560 | tf_op jit(solution)/shard_map/while/body/eval_jaxpr/ppermute | solution.py:19
  78.4 7.7 %collective-permute-start = (f32[36,12,128]{2,1,0:T(8,128)S(1)}, f32[36,12,128]{2,1,0:T(8,128)S(1)}, u32[]{:S(2)}, u32[]{:S(2)}) collective-permute-start(f32[36,12,128]{2,1,0:T(8,128)S(1)} %multiply_add_fusion.6), channel_id=1, source_target_pairs={{0,16},{16,32},{32,48},{48,64},{64,80},{80,96},{96,112},{112,128},... | collective-permute-start | bytes 663560 | tf_op jit(solution)/shard_map/while/body/eval_jaxpr/ppermute | solution.py:19
  82.5 7.5 %collective-permute-start.1 = (f32[36,12,128]{2,1,0:T(8,128)S(1)}, f32[36,12,128]{2,1,0:T(8,128)S(1)}, u32[]{:S(2)}, u32[]{:S(2)}) collective-permute-start(f32[36,12,128]{2,1,0:T(8,128)S(1)} %multiply_add_fusion.7), channel_id=1, source_target_pairs={{16,0},{32,16},{48,32},{64,48},{80,64},{96,80},{112,96},{128,112},... | collective-permute-start | bytes 663560 | tf_op jit(solution)/shard_map/while/body/eval_jaxpr/ppermute | solution.py:19
  90.1 7.7 %collective-permute-start = (f32[36,12,128]{2,1,0:T(8,128)S(1)}, f32[36,12,128]{2,1,0:T(8,128)S(1)}, u32[]{:S(2)}, u32[]{:S(2)}) collective-permute-start(f32[36,12,128]{2,1,0:T(8,128)S(1)} %multiply_add_fusion.6), channel_id=1, source_target_pairs={{0,16},{16,32},{32,48},{48,64},{64,80},{80,96},{96,112},{112,128},... | collective-permute-start | bytes 663560 | tf_op jit(solution)/shard_map/while/body/eval_jaxpr/ppermute | solution.py:19
  94.2 7.5 %collective-permute-start.1 = (f32[36,12,128]{2,1,0:T(8,128)S(1)}, f32[36,12,128]{2,1,0:T(8,128)S(1)}, u32[]{:S(2)}, u32[]{:S(2)}) collective-permute-start(f32[36,12,128]{2,1,0:T(8,128)S(1)} %multiply_add_fusion.7), channel_id=1, source_target_pairs={{16,0},{32,16},{48,32},{64,48},{80,64},{96,80},{112,96},{128,112},... | collective-permute-start | bytes 663560 | tf_op jit(solution)/shard_map/while/body/eval_jaxpr/ppermute | solution.py:19
  105.5 7.6 %collective-permute-start.1 = (f32[36,12,128]{2,1,0:T(8,128)S(1)}, f32[36,12,128]{2,1,0:T(8,128)S(1)}, u32[]{:S(2)}, u32[]{:S(2)}) collective-permute-start(f32[36,12,128]{2,1,0:T(8,128)S(1)} %multiply_add_fusion.7), channel_id=1, source_target_pairs={{16,0},{32,16},{48,32},{64,48},{80,64},{96,80},{112,96},{128,112},... | collective-permute-start | bytes 663560 | tf_op jit(solution)/shard_map/while/body/eval_jaxpr/ppermute | solution.py:19
  113.1 8.5 %collective-permute-start = (f32[36,12,128]{2,1,0:T(8,128)S(1)}, f32[36,12,128]{2,1,0:T(8,128)S(1)}, u32[]{:S(2)}, u32[]{:S(2)}) collective-permute-start(f32[36,12,128]{2,1,0:T(8,128)S(1)} %multiply_add_fusion.6), channel_id=1, source_target_pairs={{0,16},{16,32},{32,48},{48,64},{64,80},{80,96},{96,112},{112,128},... | collective-permute-start | bytes 663560 | tf_op jit(solution)/shard_map/while/body/eval_jaxpr/ppermute | solution.py:19
  117.2 8.7 %collective-permute-start.1 = (f32[36,12,128]{2,1,0:T(8,128)S(1)}, f32[36,12,128]{2,1,0:T(8,128)S(1)}, u32[]{:S(2)}, u32[]{:S(2)}) collective-permute-start(f32[36,12,128]{2,1,0:T(8,128)S(1)} %multiply_add_fusion.7), channel_id=1, source_target_pairs={{16,0},{32,16},{48,32},{64,48},{80,64},{96,80},{112,96},{128,112},... | collective-permute-start | bytes 663560 | tf_op jit(solution)/shard_map/while/body/eval_jaxpr/ppermute | solution.py:19
  125.9 9.4 %collective-permute-start = (f32[36,12,128]{2,1,0:T(8,128)S(1)}, f32[36,12,128]{2,1,0:T(8,128)S(1)}, u32[]{:S(2)}, u32[]{:S(2)}) collective-permute-start(f32[36,12,128]{2,1,0:T(8,128)S(1)} %multiply_add_fusion.6), channel_id=1, source_target_pairs={{0,16},{16,32},{32,48},{48,64},{64,80},{80,96},{96,112},{112,128},... | collective-permute-start | bytes 663560 | tf_op jit(solution)/shard_map/while/body/eval_jaxpr/ppermute | solution.py:19
  129.7 10.1 %collective-permute-start.1 = (f32[36,12,128]{2,1,0:T(8,128)S(1)}, f32[36,12,128]{2,1,0:T(8,128)S(1)}, u32[]{:S(2)}, u32[]{:S(2)}) collective-permute-start(f32[36,12,128]{2,1,0:T(8,128)S(1)} %multiply_add_fusion.7), channel_id=1, source_target_pairs={{16,0},{32,16},{48,32},{64,48},{80,64},{96,80},{112,96},{128,112},... | collective-permute-start | bytes 663560 | tf_op jit(solution)/shard_map/while/body/eval_jaxpr/ppermute | solution.py:19
  139.8 10.2 %collective-permute-start = (f32[36,12,128]{2,1,0:T(8,128)S(1)}, f32[36,12,128]{2,1,0:T(8,128)S(1)}, u32[]{:S(2)}, u32[]{:S(2)}) collective-permute-start(f32[36,12,128]{2,1,0:T(8,128)S(1)} %multiply_add_fusion.6), channel_id=1, source_target_pairs={{0,16},{16,32},{32,48},{48,64},{64,80},{80,96},{96,112},{112,128},... | collective-permute-start | bytes 663560 | tf_op jit(solution)/shard_map/while/body/eval_jaxpr/ppermute | solution.py:19
  143.6 10.7 %collective-permute-start.1 = (f32[36,12,128]{2,1,0:T(8,128)S(1)}, f32[36,12,128]{2,1,0:T(8,128)S(1)}, u32[]{:S(2)}, u32[]{:S(2)}) collective-permute-start(f32[36,12,128]{2,1,0:T(8,128)S(1)} %multiply_add_fusion.7), channel_id=1, source_target_pairs={{16,0},{32,16},{48,32},{64,48},{80,64},{96,80},{112,96},{128,112},... | collective-permute-start | bytes 663560 | tf_op jit(solution)/shard_map/while/body/eval_jaxpr/ppermute | solution.py:19
  154.3 9.5 %collective-permute-start = (f32[36,12,128]{2,1,0:T(8,128)S(1)}, f32[36,12,128]{2,1,0:T(8,128)S(1)}, u32[]{:S(2)}, u32[]{:S(2)}) collective-permute-start(f32[36,12,128]{2,1,0:T(8,128)S(1)} %multiply_add_fusion.6), channel_id=1, source_target_pairs={{0,16},{16,32},{32,48},{48,64},{64,80},{80,96},{96,112},{112,128},... | collective-permute-start | bytes 663560 | tf_op jit(solution)/shard_map/while/body/eval_jaxpr/ppermute | solution.py:19
  158.3 9.5 %collective-permute-start.1 = (f32[36,12,128]{2,1,0:T(8,128)S(1)}, f32[36,12,128]{2,1,0:T(8,128)S(1)}, u32[]{:S(2)}, u32[]{:S(2)}) collective-permute-start(f32[36,12,128]{2,1,0:T(8,128)S(1)} %multiply_add_fusion.7), channel_id=1, source_target_pairs={{16,0},{32,16},{48,32},{64,48},{80,64},{96,80},{112,96},{128,112},... | collective-permute-start | bytes 663560 | tf_op jit(solution)/shard_map/while/body/eval_jaxpr/ppermute | solution.py:19
  167.8 9.9 %collective-permute-start = (f32[36,12,128]{2,1,0:T(8,128)S(1)}, f32[36,12,128]{2,1,0:T(8,128)S(1)}, u32[]{:S(2)}, u32[]{:S(2)}) collective-permute-start(f32[36,12,128]{2,1,0:T(8,128)S(1)} %multiply_add_fusion.6), channel_id=1, source_target_pairs={{0,16},{16,32},{32,48},{48,64},{64,80},{80,96},{96,112},{112,128},... | collective-permute-start | bytes 663560 | tf_op jit(solution)/shard_map/while/body/eval_jaxpr/ppermute | solution.py:19
  172.7 8.9 %collective-permute-start.1 = (f32[36,12,128]{2,1,0:T(8,128)S(1)}, f32[36,12,128]{2,1,0:T(8,128)S(1)}, u32[]{:S(2)}, u32[]{:S(2)}) collective-permute-start(f32[36,12,128]{2,1,0:T(8,128)S(1)} %multiply_add_fusion.7), channel_id=1, source_target_pairs={{16,0},{32,16},{48,32},{64,48},{80,64},{96,80},{112,96},{128,112},... | collective-permute-start | bytes 663560 | tf_op jit(solution)/shard_map/while/body/eval_jaxpr/ppermute | solution.py:19
  181.7 8.4 %collective-permute-start = (f32[36,12,128]{2,1,0:T(8,128)S(1)}, f32[36,12,128]{2,1,0:T(8,128)S(1)}, u32[]{:S(2)}, u32[]{:S(2)}) collective-permute-start(f32[36,12,128]{2,1,0:T(8,128)S(1)} %multiply_add_fusion.6), channel_id=1, source_target_pairs={{0,16},{16,32},{32,48},{48,64},{64,80},{80,96},{96,112},{112,128},... | collective-permute-start | bytes 663560 | tf_op jit(solution)/shard_map/while/body/eval_jaxpr/ppermute | solution.py:19
  186.0 8.0 %collective-permute-start.1 = (f32[36,12,128]{2,1,0:T(8,128)S(1)}, f32[36,12,128]{2,1,0:T(8,128)S(1)}, u32[]{:S(2)}, u32[]{:S(2)}) collective-permute-start(f32[36,12,128]{2,1,0:T(8,128)S(1)} %multiply_add_fusion.7), channel_id=1, source_target_pairs={{16,0},{32,16},{48,32},{64,48},{80,64},{96,80},{112,96},{128,112},... | collective-permute-start | bytes 663560 | tf_op jit(solution)/shard_map/while/body/eval_jaxpr/ppermute | solution.py:19
  194.1 8.0 %collective-permute-start = (f32[36,12,128]{2,1,0:T(8,128)S(1)}, f32[36,12,128]{2,1,0:T(8,128)S(1)}, u32[]{:S(2)}, u32[]{:S(2)}) collective-permute-start(f32[36,12,128]{2,1,0:T(8,128)S(1)} %multiply_add_fusion.6), channel_id=1, source_target_pairs={{0,16},{16,32},{32,48},{48,64},{64,80},{80,96},{96,112},{112,128},... | collective-permute-start | bytes 663560 | tf_op jit(solution)/shard_map/while/body/eval_jaxpr/ppermute | solution.py:19
  206.0 7.7 %collective-permute-start = (f32[36,12,128]{2,1,0:T(8,128)S(1)}, f32[36,12,128]{2,1,0:T(8,128)S(1)}, u32[]{:S(2)}, u32[]{:S(2)}) collective-permute-start(f32[36,12,128]{2,1,0:T(8,128)S(1)} %multiply_add_fusion.6), channel_id=1, source_target_pairs={{0,16},{16,32},{32,48},{48,64},{64,80},{80,96},{96,112},{112,128},... | collective-permute-start | bytes 663560 | tf_op jit(solution)/shard_map/while/body/eval_jaxpr/ppermute | solution.py:19
  217.6 8.0 %collective-permute-start = (f32[36,12,128]{2,1,0:T(8,128)S(1)}, f32[36,12,128]{2,1,0:T(8,128)S(1)}, u32[]{:S(2)}, u32[]{:S(2)}) collective-permute-start(f32[36,12,128]{2,1,0:T(8,128)S(1)} %multiply_add_fusion.6), channel_id=1, source_target_pairs={{0,16},{16,32},{32,48},{48,64},{64,80},{80,96},{96,112},{112,128},... | collective-permute-start | bytes 663560 | tf_op jit(solution)/shard_map/while/body/eval_jaxpr/ppermute | solution.py:19
  (21 other events, 142.0 us)
where the time goes:
time: 532 us; the launch traced here: 530 us
  blocking collectives  260 us (49%)
  waiting for transfers between devices  116 us (22%)
  starting transfers between devices  100 us (19%)
  between operations  16.2 us (3%)
  local copies, waits for them, and re-layouts  15.9 us (3%)
  other arithmetic  14.6 us (3%)
  matrix products  6.31 us (1%)
    psum x2, blocking collectives, body(): lax.psum(newton_sums(loaded, signed, shift_mass, shift_flow), ('sec', 've...  157 us
    ppermute x30, waiting for transfers between devices, passed_along(): return lax.ppermute(block, axis, route)  104 us
    ppermute x30, starting transfers between devices, passed_along(): return lax.ppermute(block, axis, route)  79.3 us
    psum x1, blocking collectives, body(): lax.psum(jnp.dot(weighted, half_field, precision=HIGH), 'vel')  44.9 us
    psum x1, blocking collectives, body(): goals = lax.psum(local_totals, 'sec')  30.6 us
    psum x1, blocking collectives, body(): lax.psum(jnp.dot(weighted, distribution, precision=HIGH), 'vel')  27.9 us
    ppermute x4, starting transfers between devices, extended(): before = lax.ppermute(last, axis, up)  15.5 us
    ppermute x4, waiting for transfers between devices, extended(): after = lax.ppermute(first, axis, down)  12.3 us
  transfers between devices with their start and end apart: 38, of which 34 were waited for; matrix products, arithmetic and copies ran while one was open for 0% of the time, Pallas kernels for 0%

commit v1 on v0

--- a/solution.py
+++ b/solution.py
@@ -191,7 +191,7 @@
     goals = lax.psum(local_totals, "sec")
     loaded = node_mass * magnitude
     for newton_turn in range(NEWTON):
-        sums = lax.psum(newton_sums(loaded, signed, shift_mass, shift_flow), ("sec", "vel"))
+        sums = lax.psum(lax.psum(newton_sums(loaded, signed, shift_mass, shift_flow), "sec"), "vel")
         shift_mass, shift_flow = newton_update(shift_mass, shift_flow, sums, goals[0], goals[1])
     growth = jnp.exp(shift_mass + shift_flow * signed)
     new_distribution = synthetic + jnp.abs(synthetic) * (growth[:, None] - 1.0)

time: 532 us -> 469 us (0.88)
  blocking collectives: 260 us -> 197 us
    psum x3 -> x4, blocking collectives: 188 us -> 124 us  [the longest x2 65.4 us: body(): lax.psum(lax.psum(newton_sums(loaded, signed, shift_mass, shift_flow), 's...]
where the time goes in v1:
time: 469 us; the launch traced here: 467 us
  blocking collectives  197 us (42%)
  waiting for transfers between devices  116 us (25%)
  starting transfers between devices  100 us (21%)
  between operations  16.2 us (3%)
  local copies, waits for them, and re-layouts  16 us (3%)
  other arithmetic  14.6 us (3%)
  matrix products  6.31 us (1%)
    ppermute x30, waiting for transfers between devices, passed_along(): return lax.ppermute(block, axis, route)  104 us
    ppermute x30, starting transfers between devices, passed_along(): return lax.ppermute(block, axis, route)  79.3 us
    psum x2, blocking collectives, body(): lax.psum(lax.psum(newton_sums(loaded, signed, shift_mass, shift_flow), 's...  65.4 us
    psum x2, blocking collectives, body(): lax.psum(newton_sums(loaded, signed, shift_mass, shift_flow), 'sec')  59.1 us
    psum x1, blocking collectives, body(): lax.psum(jnp.dot(weighted, half_field, precision=HIGH), 'vel')  44.9 us
    psum x1, blocking collectives, body(): lax.psum(jnp.dot(weighted, distribution, precision=HIGH), 'vel')  27.9 us
    ppermute x4, starting transfers between devices, extended(): before = lax.ppermute(last, axis, up)  15.5 us
    ppermute x4, waiting for transfers between devices, extended(): after = lax.ppermute(first, axis, down)  12.3 us
  transfers between devices with their start and end apart: 38, of which 34 were waited for; matrix products, arithmetic and copies ran while one was open for 0% of the time, Pallas kernels for 0%

profile of v1, /device:TPU:1, one launch (start us, length us, event | category | flops | bytes accessed | tf_op | source)
XLA Modules:
  0.0 466.8 jit_solution(12689609594375236476)
XLA Ops:
  3.6 27.9 %psum.49 = f32[5,256]{1,0:T(8,128)S(1)} all-reduce(f32[5,256]{1,0:T(8,128)S(1)} %fusion.12), channel_id=1, replica_groups=mesh['sec'=16,'vel'=16] {'vel'}, use_global_device_ids=true, to_apply=%region_0.0 | all-reduce | flops 1280 | bytes 10240 | tf_op jit(solution)/shard_map/psum | solution.py:139
  44.4 185.1 %while.12 = (s32[]{:T(128)}, f32[36,12,128]{2,1,0:T(8,128)S(1)}, f32[36,12,128]{2,1,0:T(8,128)S(1)}, f32[36,12,128]{2,1,0:T(8,128)S(1)}, f32[36,12,128]{2,1,0:T(...) while((s32[]{:T(128)}, f32[36,12,128]{2,1,0:T(8,128)S(1)}, ...), condition=%wide.region_2.0_spmd, body=%wide.region_1.0_spmd.sunk | while | flops 221186 | bytes 3539109 | solution.py:168
  66.4 4.4 collective-permute-start
  78.4 4.0 collective-permute-start
  90.1 4.0 collective-permute-start
  109.1 4.0 collective-permute-done.1
  121.7 4.2 collective-permute-done.1
  131.0 4.3 collective-permute-done
  135.3 4.4 collective-permute-done.1
  144.9 5.2 %collective-permute-done = f32[36,12,128]{2,1,0:T(8,128)S(1)} collective-permute-done((f32[36,12,128]{2,1,0:T(8,128)S(1)}, f32[36,12,128]{2,1,0:T(8,128)S(1)}, u32[]{:S(2)}, u32[]{:S(2)}) %collective-permute-start) | collective-permute-done | bytes 221216 | tf_op jit(solution)/shard_map/while/body/eval_jaxpr/ppermute | solution.py:19
  150.1 4.2 collective-permute-done.1
  159.6 4.3 collective-permute-done
  167.8 4.8 %collective-permute-start = (f32[36,12,128]{2,1,0:T(8,128)S(1)}, f32[36,12,128]{2,1,0:T(8,128)S(1)}, u32[]{:S(2)}, u32[]{:S(2)}) collective-permute-start(f32[36,12,128]{2,1,0:T(8,128)S(1)} %multiply_add_fusion.6), channel_id=1, source_target_pairs={{0,16},{16,32},{32,48},{48,64},{64,80},{80,96},{96,112},{112,128},... | collective-permute-start | bytes 663560 | tf_op jit(solution)/shard_map/while/body/eval_jaxpr/ppermute | solution.py:19
  181.7 4.3 collective-permute-start
  194.1 4.3 collective-permute-start
  206.0 4.0 collective-permute-start
  217.6 4.3 collective-permute-start
  232.6 44.9 %psum.50 = f32[5,256]{1,0:T(8,128)S(1)} all-reduce(f32[5,256]{1,0:T(8,128)S(1)} %fusion), channel_id=1, replica_groups=mesh['sec'=16,'vel'=16] {'vel'}, use_global_device_ids=true, to_apply=%region_3.0 | all-reduce | flops 1280 | bytes 10240 | tf_op jit(solution)/shard_map/psum | solution.py:172
  294.3 4.0 collective-permute-start.6
  302.8 4.0 collective-permute-start.8
  318.7 30.6 %all-reduce.8 = (f32[5]{0:T(128)S(1)}, f32[2]{0:T(128)S(1)}) all-reduce(f32[5]{0:T(128)S(1)} %stack.41, f32[2]{0:T(128)S(1)} %bitcast.57), channel_id=1, replica_groups=mesh['sec'=16,'vel'=16] {'sec'}, use_global_device_ids=true, to_apply=%region_23.0 | all-reduce | flops 7 | bytes 56 | tf_op jit(solution)/shard_map/psum | solution.py:194
  349.3 34.9 %psum.52 = f32[5]{0:T(128)S(1)} all-reduce(f32[5]{0:T(128)S(1)} %get-tuple-element.73), channel_id=1, replica_groups=mesh['sec'=16,'vel'=16] {'vel'}, use_global_device_ids=true, to_apply=%region_24.0 | all-reduce | flops 5 | bytes 40 | tf_op jit(solution)/shard_map/psum | solution.py:194
  397.8 28.5 %psum.54 = f32[5]{0:T(128)S(1)} all-reduce(f32[5]{0:T(128)S(1)} %stack.47), channel_id=1, replica_groups=mesh['sec'=16,'vel'=16] {'sec'}, use_global_device_ids=true, to_apply=%region_32.0 | all-reduce | flops 5 | bytes 40 | tf_op jit(solution)/shard_map/psum | solution.py:194
  426.2 30.5 %psum.55 = f32[5]{0:T(128)S(1)} all-reduce(f32[5]{0:T(128)S(1)} %psum.54), channel_id=1, replica_groups=mesh['sec'=16,'vel'=16] {'vel'}, use_global_device_ids=true, to_apply=%region_33.0 | all-reduce | flops 5 | bytes 40 | tf_op jit(solution)/shard_map/psum | solution.py:194
  (167 shorter events, 179.8 us)
Async XLA Ops:
  47.8 7.5 %collective-permute-start.1 = (f32[36,12,128]{2,1,0:T(8,128)S(1)}, f32[36,12,128]{2,1,0:T(8,128)S(1)}, u32[]{:S(2)}, u32[]{:S(2)}) collective-permute-start(f32[36,12,128]{2,1,0:T(8,128)S(1)} %multiply_add_fusion.7), channel_id=1, source_target_pairs={{16,0},{32,16},{48,32},{64,48},{80,64},{96,80},{112,96},{128,112},... | collective-permute-start | bytes 663560 | tf_op jit(solution)/shard_map/while/body/eval_jaxpr/ppermute | solution.py:19
  58.9 7.5 %collective-permute-start.1 = (f32[36,12,128]{2,1,0:T(8,128)S(1)}, f32[36,12,128]{2,1,0:T(8,128)S(1)}, u32[]{:S(2)}, u32[]{:S(2)}) collective-permute-start(f32[36,12,128]{2,1,0:T(8,128)S(1)} %multiply_add_fusion.7), channel_id=1, source_target_pairs={{16,0},{32,16},{48,32},{64,48},{80,64},{96,80},{112,96},{128,112},... | collective-permute-start | bytes 663560 | tf_op jit(solution)/shard_map/while/body/eval_jaxpr/ppermute | solution.py:19
  66.4 8.1 %collective-permute-start = (f32[36,12,128]{2,1,0:T(8,128)S(1)}, f32[36,12,128]{2,1,0:T(8,128)S(1)}, u32[]{:S(2)}, u32[]{:S(2)}) collective-permute-start(f32[36,12,128]{2,1,0:T(8,128)S(1)} %multiply_add_fusion.6), channel_id=1, source_target_pairs={{0,16},{16,32},{32,48},{48,64},{64,80},{80,96},{96,112},{112,128},... | collective-permute-start | bytes 663560 | tf_op jit(solution)/shard_map/while/body/eval_jaxpr/ppermute | solution.py:19
  70.9 7.5 %collective-permute-start.1 = (f32[36,12,128]{2,1,0:T(8,128)S(1)}, f32[36,12,128]{2,1,0:T(8,128)S(1)}, u32[]{:S(2)}, u32[]{:S(2)}) collective-permute-start(f32[36,12,128]{2,1,0:T(8,128)S(1)} %multiply_add_fusion.7), channel_id=1, source_target_pairs={{16,0},{32,16},{48,32},{64,48},{80,64},{96,80},{112,96},{128,112},... | collective-permute-start | bytes 663560 | tf_op jit(solution)/shard_map/while/body/eval_jaxpr/ppermute | solution.py:19
  78.4 7.7 %collective-permute-start = (f32[36,12,128]{2,1,0:T(8,128)S(1)}, f32[36,12,128]{2,1,0:T(8,128)S(1)}, u32[]{:S(2)}, u32[]{:S(2)}) collective-permute-start(f32[36,12,128]{2,1,0:T(8,128)S(1)} %multiply_add_fusion.6), channel_id=1, source_target_pairs={{0,16},{16,32},{32,48},{48,64},{64,80},{80,96},{96,112},{112,128},... | collective-permute-start | bytes 663560 | tf_op jit(solution)/shard_map/while/body/eval_jaxpr/ppermute | solution.py:19
  82.5 7.5 %collective-permute-start.1 = (f32[36,12,128]{2,1,0:T(8,128)S(1)}, f32[36,12,128]{2,1,0:T(8,128)S(1)}, u32[]{:S(2)}, u32[]{:S(2)}) collective-permute-start(f32[36,12,128]{2,1,0:T(8,128)S(1)} %multiply_add_fusion.7), channel_id=1, source_target_pairs={{16,0},{32,16},{48,32},{64,48},{80,64},{96,80},{112,96},{128,112},... | collective-permute-start | bytes 663560 | tf_op jit(solution)/shard_map/while/body/eval_jaxpr/ppermute | solution.py:19
  90.1 7.7 %collective-permute-start = (f32[36,12,128]{2,1,0:T(8,128)S(1)}, f32[36,12,128]{2,1,0:T(8,128)S(1)}, u32[]{:S(2)}, u32[]{:S(2)}) collective-permute-start(f32[36,12,128]{2,1,0:T(8,128)S(1)} %multiply_add_fusion.6), channel_id=1, source_target_pairs={{0,16},{16,32},{32,48},{48,64},{64,80},{80,96},{96,112},{112,128},... | collective-permute-start | bytes 663560 | tf_op jit(solution)/shard_map/while/body/eval_jaxpr/ppermute | solution.py:19
  94.2 7.5 %collective-permute-start.1 = (f32[36,12,128]{2,1,0:T(8,128)S(1)}, f32[36,12,128]{2,1,0:T(8,128)S(1)}, u32[]{:S(2)}, u32[]{:S(2)}) collective-permute-start(f32[36,12,128]{2,1,0:T(8,128)S(1)} %multiply_add_fusion.7), channel_id=1, source_target_pairs={{16,0},{32,16},{48,32},{64,48},{80,64},{96,80},{112,96},{128,112},... | collective-permute-start | bytes 663560 | tf_op jit(solution)/shard_map/while/body/eval_jaxpr/ppermute | solution.py:19
  105.5 7.6 %collective-permute-start.1 = (f32[36,12,128]{2,1,0:T(8,128)S(1)}, f32[36,12,128]{2,1,0:T(8,128)S(1)}, u32[]{:S(2)}, u32[]{:S(2)}) collective-permute-start(f32[36,12,128]{2,1,0:T(8,128)S(1)} %multiply_add_fusion.7), channel_id=1, source_target_pairs={{16,0},{32,16},{48,32},{64,48},{80,64},{96,80},{112,96},{128,112},... | collective-permute-start | bytes 663560 | tf_op jit(solution)/shard_map/while/body/eval_jaxpr/ppermute | solution.py:19
  113.1 8.5 %collective-permute-start = (f32[36,12,128]{2,1,0:T(8,128)S(1)}, f32[36,12,128]{2,1,0:T(8,128)S(1)}, u32[]{:S(2)}, u32[]{:S(2)}) collective-permute-start(f32[36,12,128]{2,1,0:T(8,128)S(1)} %multiply_add_fusion.6), channel_id=1, source_target_pairs={{0,16},{16,32},{32,48},{48,64},{64,80},{80,96},{96,112},{112,128},... | collective-permute-start | bytes 663560 | tf_op jit(solution)/shard_map/while/body/eval_jaxpr/ppermute | solution.py:19
  117.2 8.7 %collective-permute-start.1 = (f32[36,12,128]{2,1,0:T(8,128)S(1)}, f32[36,12,128]{2,1,0:T(8,128)S(1)}, u32[]{:S(2)}, u32[]{:S(2)}) collective-permute-start(f32[36,12,128]{2,1,0:T(8,128)S(1)} %multiply_add_fusion.7), channel_id=1, source_target_pairs={{16,0},{32,16},{48,32},{64,48},{80,64},{96,80},{112,96},{128,112},... | collective-permute-start | bytes 663560 | tf_op jit(solution)/shard_map/while/body/eval_jaxpr/ppermute | solution.py:19
  125.9 9.4 %collective-permute-start = (f32[36,12,128]{2,1,0:T(8,128)S(1)}, f32[36,12,128]{2,1,0:T(8,128)S(1)}, u32[]{:S(2)}, u32[]{:S(2)}) collective-permute-start(f32[36,12,128]{2,1,0:T(8,128)S(1)} %multiply_add_fusion.6), channel_id=1, source_target_pairs={{0,16},{16,32},{32,48},{48,64},{64,80},{80,96},{96,112},{112,128},... | collective-permute-start | bytes 663560 | tf_op jit(solution)/shard_map/while/body/eval_jaxpr/ppermute | solution.py:19
  129.7 10.1 %collective-permute-start.1 = (f32[36,12,128]{2,1,0:T(8,128)S(1)}, f32[36,12,128]{2,1,0:T(8,128)S(1)}, u32[]{:S(2)}, u32[]{:S(2)}) collective-permute-start(f32[36,12,128]{2,1,0:T(8,128)S(1)} %multiply_add_fusion.7), channel_id=1, source_target_pairs={{16,0},{32,16},{48,32},{64,48},{80,64},{96,80},{112,96},{128,112},... | collective-permute-start | bytes 663560 | tf_op jit(solution)/shard_map/while/body/eval_jaxpr/ppermute | solution.py:19
  139.8 10.2 %collective-permute-start = (f32[36,12,128]{2,1,0:T(8,128)S(1)}, f32[36,12,128]{2,1,0:T(8,128)S(1)}, u32[]{:S(2)}, u32[]{:S(2)}) collective-permute-start(f32[36,12,128]{2,1,0:T(8,128)S(1)} %multiply_add_fusion.6), channel_id=1, source_target_pairs={{0,16},{16,32},{32,48},{48,64},{64,80},{80,96},{96,112},{112,128},... | collective-permute-start | bytes 663560 | tf_op jit(solution)/shard_map/while/body/eval_jaxpr/ppermute | solution.py:19
  143.6 10.7 %collective-permute-start.1 = (f32[36,12,128]{2,1,0:T(8,128)S(1)}, f32[36,12,128]{2,1,0:T(8,128)S(1)}, u32[]{:S(2)}, u32[]{:S(2)}) collective-permute-start(f32[36,12,128]{2,1,0:T(8,128)S(1)} %multiply_add_fusion.7), channel_id=1, source_target_pairs={{16,0},{32,16},{48,32},{64,48},{80,64},{96,80},{112,96},{128,112},... | collective-permute-start | bytes 663560 | tf_op jit(solution)/shard_map/while/body/eval_jaxpr/ppermute | solution.py:19
  154.3 9.5 %collective-permute-start = (f32[36,12,128]{2,1,0:T(8,128)S(1)}, f32[36,12,128]{2,1,0:T(8,128)S(1)}, u32[]{:S(2)}, u32[]{:S(2)}) collective-permute-start(f32[36,12,128]{2,1,0:T(8,128)S(1)} %multiply_add_fusion.6), channel_id=1, source_target_pairs={{0,16},{16,32},{32,48},{48,64},{64,80},{80,96},{96,112},{112,128},... | collective-permute-start | bytes 663560 | tf_op jit(solution)/shard_map/while/body/eval_jaxpr/ppermute | solution.py:19
  158.3 9.5 %collective-permute-start.1 = (f32[36,12,128]{2,1,0:T(8,128)S(1)}, f32[36,12,128]{2,1,0:T(8,128)S(1)}, u32[]{:S(2)}, u32[]{:S(2)}) collective-permute-start(f32[36,12,128]{2,1,0:T(8,128)S(1)} %multiply_add_fusion.7), channel_id=1, source_target_pairs={{16,0},{32,16},{48,32},{64,48},{80,64},{96,80},{112,96},{128,112},... | collective-permute-start | bytes 663560 | tf_op jit(solution)/shard_map/while/body/eval_jaxpr/ppermute | solution.py:19
  167.8 9.9 %collective-permute-start = (f32[36,12,128]{2,1,0:T(8,128)S(1)}, f32[36,12,128]{2,1,0:T(8,128)S(1)}, u32[]{:S(2)}, u32[]{:S(2)}) collective-permute-start(f32[36,12,128]{2,1,0:T(8,128)S(1)} %multiply_add_fusion.6), channel_id=1, source_target_pairs={{0,16},{16,32},{32,48},{48,64},{64,80},{80,96},{96,112},{112,128},... | collective-permute-start | bytes 663560 | tf_op jit(solution)/shard_map/while/body/eval_jaxpr/ppermute | solution.py:19
  172.7 8.9 %collective-permute-start.1 = (f32[36,12,128]{2,1,0:T(8,128)S(1)}, f32[36,12,128]{2,1,0:T(8,128)S(1)}, u32[]{:S(2)}, u32[]{:S(2)}) collective-permute-start(f32[36,12,128]{2,1,0:T(8,128)S(1)} %multiply_add_fusion.7), channel_id=1, source_target_pairs={{16,0},{32,16},{48,32},{64,48},{80,64},{96,80},{112,96},{128,112},... | collective-permute-start | bytes 663560 | tf_op jit(solution)/shard_map/while/body/eval_jaxpr/ppermute | solution.py:19
  181.7 8.4 %collective-permute-start = (f32[36,12,128]{2,1,0:T(8,128)S(1)}, f32[36,12,128]{2,1,0:T(8,128)S(1)}, u32[]{:S(2)}, u32[]{:S(2)}) collective-permute-start(f32[36,12,128]{2,1,0:T(8,128)S(1)} %multiply_add_fusion.6), channel_id=1, source_target_pairs={{0,16},{16,32},{32,48},{48,64},{64,80},{80,96},{96,112},{112,128},... | collective-permute-start | bytes 663560 | tf_op jit(solution)/shard_map/while/body/eval_jaxpr/ppermute | solution.py:19
  186.0 8.0 %collective-permute-start.1 = (f32[36,12,128]{2,1,0:T(8,128)S(1)}, f32[36,12,128]{2,1,0:T(8,128)S(1)}, u32[]{:S(2)}, u32[]{:S(2)}) collective-permute-start(f32[36,12,128]{2,1,0:T(8,128)S(1)} %multiply_add_fusion.7), channel_id=1, source_target_pairs={{16,0},{32,16},{48,32},{64,48},{80,64},{96,80},{112,96},{128,112},... | collective-permute-start | bytes 663560 | tf_op jit(solution)/shard_map/while/body/eval_jaxpr/ppermute | solution.py:19
  194.1 8.0 %collective-permute-start = (f32[36,12,128]{2,1,0:T(8,128)S(1)}, f32[36,12,128]{2,1,0:T(8,128)S(1)}, u32[]{:S(2)}, u32[]{:S(2)}) collective-permute-start(f32[36,12,128]{2,1,0:T(8,128)S(1)} %multiply_add_fusion.6), channel_id=1, source_target_pairs={{0,16},{16,32},{32,48},{48,64},{64,80},{80,96},{96,112},{112,128},... | collective-permute-start | bytes 663560 | tf_op jit(solution)/shard_map/while/body/eval_jaxpr/ppermute | solution.py:19
  206.0 7.7 %collective-permute-start = (f32[36,12,128]{2,1,0:T(8,128)S(1)}, f32[36,12,128]{2,1,0:T(8,128)S(1)}, u32[]{:S(2)}, u32[]{:S(2)}) collective-permute-start(f32[36,12,128]{2,1,0:T(8,128)S(1)} %multiply_add_fusion.6), channel_id=1, source_target_pairs={{0,16},{16,32},{32,48},{48,64},{64,80},{80,96},{96,112},{112,128},... | collective-permute-start | bytes 663560 | tf_op jit(solution)/shard_map/while/body/eval_jaxpr/ppermute | solution.py:19
  217.6 8.0 %collective-permute-start = (f32[36,12,128]{2,1,0:T(8,128)S(1)}, f32[36,12,128]{2,1,0:T(8,128)S(1)}, u32[]{:S(2)}, u32[]{:S(2)}) collective-permute-start(f32[36,12,128]{2,1,0:T(8,128)S(1)} %multiply_add_fusion.6), channel_id=1, source_target_pairs={{0,16},{16,32},{32,48},{48,64},{64,80},{80,96},{96,112},{112,128},... | collective-permute-start | bytes 663560 | tf_op jit(solution)/shard_map/while/body/eval_jaxpr/ppermute | solution.py:19
  (21 other events, 142.0 us)
